TPU v7x, 512 devices: a whole 4x8x8 slice. The times are simulated.
512 devices in a mesh: ctx: 32 (over y_lo, z, core), tp: 16 (over x, y_hi).
Axes of the slice: x: 4, y: 8 (y_hi: 4, y_lo: 2; y = y_hi * 2 + y_lo), z: 8, core: 2. Of those that a mesh axis runs over, the one named last changes fastest.
Arguments:
- query: bfloat16 [8192, 4096], P('ctx', 'tp'), may hold values from 0.049804688 to 2
- key_feat: bfloat16 [8192, 4096], P('ctx', 'tp'), may hold values from 0.049804688 to 2
- value: bfloat16 [8192, 4096], P('ctx', 'tp'), may hold values from -36 to 36
- grad_out: bfloat16 [8192, 4096], P('ctx', 'tp'), may hold values from -6 to 6
- w_out: bfloat16 [4096, 4096], P('tp', 'ctx'), may hold values from -0.09375 to 0.09375
Outputs:
- grad_query: bfloat16 [8192, 4096], P('ctx', 'tp')
- grad_key: bfloat16 [8192, 4096], P('ctx', 'tp')
- grad_value: bfloat16 [8192, 4096], P('ctx', 'tp')
All inputs are finite; a program needn't handle non-finite values.
Results may differ from a plain program's by a relative error of at most 0.0059.
Values may be sent and summed in bfloat16 or wider, within the bound.
No kernel may reach another device: no remote copies, remote signals or barrier semaphores. Data moves between devices by JAX's collectives and lax.ppermute only.
A program may use at most 64 MiB of HBM per device.

v0:
```python
import jax
import jax.numpy as jnp
from jax import lax
from jax.sharding import Mesh
from jax.sharding import PartitionSpec as P

E = 128
epsilon = 1e-06
highest = lax.Precision.HIGHEST
CTX = ("ylo", "z", "core")
TP = ("x", "yhi")
CHIPS = ("ylo", "z")


def swap_cores(value):
    return lax.ppermute(value, "core", [(0, 1), (1, 0)])


def ctx_scan(local_state, backward):
    core = lax.axis_index("core")
    other = swap_cores(local_state)
    first = jnp.where(core == 0, local_state, other)
    second = jnp.where(core == 0, other, local_state)
    chip_total = first + second
    if backward:
        within = jnp.where(core == 0, other, jnp.zeros_like(other))
    else:
        within = jnp.where(core == 1, other, jnp.zeros_like(other))
    half = lax.dynamic_index_in_dim(chip_total, core, 0, keepdims=False)
    chips = lax.axis_size("ylo") * lax.axis_size("z")
    window = half
    below = jnp.zeros_like(half)
    distance = 1
    while distance < chips:
        if backward:
            pairs = [(q, q - distance) for q in range(distance, chips)]
        else:
            pairs = [(q, q + distance) for q in range(chips - distance)]
        arrived = lax.ppermute(window, CHIPS, pairs)
        below = below + arrived
        if distance * 2 < chips:
            window = window + arrived
        distance *= 2
    other_half = swap_cores(below)
    head0 = jnp.where(core == 0, below, other_half)
    head1 = jnp.where(core == 0, other_half, below)
    return jnp.stack([head0, head1]) + within


def local(query, key_feat, value, grad_out, w_out):
    tok_rows = query.shape[0]
    feat_width = query.shape[1]
    head_count = feat_width // E
    full_rows = lax.all_gather(grad_out, TP, axis=1, tiled=True)
    grad_z = lax.dot_general(
        full_rows,
        lax.all_gather(w_out, CTX, axis=1, tiled=True),
        (((1,), (1,)), ((), ())),
        preferred_element_type=jnp.float32,
    )
    query_heads = query.reshape(tok_rows, head_count, E)
    key_heads = key_feat.reshape(tok_rows, head_count, E)
    value_heads = value.reshape(tok_rows, head_count, E)
    gradz_heads = grad_z.reshape(tok_rows, head_count, E)
    query_wide = query_heads.astype(jnp.float32)
    key_wide = key_heads.astype(jnp.float32)
    value_wide = value_heads.astype(jnp.float32)
    causal = (
        lax.broadcasted_iota(jnp.int32, (tok_rows, tok_rows), 0)
        >= lax.broadcasted_iota(jnp.int32, (tok_rows, tok_rows), 1)
    )[None]
    scores = jnp.einsum("thd,shd->hts", query_heads, key_heads, preferred_element_type=jnp.float32)
    weights = jnp.where(causal, scores, 0.0)
    local_state = jnp.einsum(
        "shd,she->hde", key_heads, value_heads, preferred_element_type=jnp.float32
    )
    state_in = ctx_scan(local_state, False)
    attended = jnp.einsum("hts,she->the", weights, value_wide, precision=highest)
    attended = attended + jnp.einsum("thd,hde->the", query_wide, state_in, precision=highest)
    inv_rms = lax.rsqrt(jnp.mean(attended * attended, axis=-1, keepdims=True) + epsilon)
    normed = attended * inv_rms
    grad_att = (
        inv_rms * (gradz_heads - normed * jnp.mean(gradz_heads * normed, axis=-1, keepdims=True))
    ).astype(jnp.bfloat16)
    grad_wide = grad_att.astype(jnp.float32)
    grad_weights = jnp.where(
        causal,
        jnp.einsum("the,she->hts", grad_att, value_heads, preferred_element_type=jnp.float32),
        0.0,
    )
    grad_query = jnp.einsum("hts,shd->thd", grad_weights, key_wide, precision=highest)
    grad_query = grad_query + jnp.einsum("the,hde->thd", grad_wide, state_in, precision=highest)
    local_adjoint = jnp.einsum(
        "thd,the->hde", query_heads, grad_att, preferred_element_type=jnp.float32
    )
    adjoint = ctx_scan(local_adjoint, True)
    grad_key = jnp.einsum("hts,thd->shd", grad_weights, query_wide, precision=highest)
    grad_key = grad_key + jnp.einsum("she,hde->shd", value_wide, adjoint, precision=highest)
    grad_value = jnp.einsum("hts,the->she", weights, grad_wide, precision=highest)
    grad_value = grad_value + jnp.einsum("shd,hde->she", key_wide, adjoint, precision=highest)
    return (
        grad_query.reshape(tok_rows, feat_width).astype(jnp.bfloat16),
        grad_key.reshape(tok_rows, feat_width).astype(jnp.bfloat16),
        grad_value.reshape(tok_rows, feat_width).astype(jnp.bfloat16),
    )


def solution(mesh):
    ctx_size, tp_size = mesh.devices.shape
    chips_y = 2
    fine = Mesh(
        mesh.devices.reshape(chips_y, ctx_size // (2 * chips_y), 2, tp_size // 4, 4), CTX + TP
    )
    return jax.shard_map(
        local,
        mesh=fine,
        in_specs=(P(CTX, TP), P(CTX, TP), P(CTX, TP), P(CTX, TP), P(TP, CTX)),
        out_specs=(P(CTX, TP), P(CTX, TP), P(CTX, TP)),
        check_vma=False,
    )
```

profile of v0, /device:TPU:3, one launch (start us, length us, event | category | flops | bytes accessed | tf_op | source)
XLA Modules:
  0.0 203.0 jit_solution(1962932447259268916)
XLA Ops:
  7.2 0.0 copy-start
  7.2 0.0 copy-start.1
  7.2 0.0 all-gather.3.cloned.1.call-start
  7.2 0.7 all-gather.3.cloned.1.call-update
  7.9 0.0 all-gather.5.cloned.1.call-start
  8.0 0.7 all-gather.5.cloned.1.call-update
  8.7 1.0 copy.76
  9.7 1.1 fusion.9
  10.8 2.6 %collective-permute-start = (f32[2,128,128]{2,1,0:T(8,128)S(1)}, f32[2,128,128]{2,1,0:T(8,128)S(1)}, u32[]{:S(2)}, u32[]{:S(2)}) collective-permute-start(f32[2,128,128]{2,1,0:T(8,128)S(1)} %fusion.9), channel_id=1, source_target_pairs={{0,16},{16,0},{1,17},{17,1},{2,18},{18,2},{3,19},{19,3},{4,20},{20... | collective-permute-start | bytes 393224 | tf_op jit(solution)/shard_map/ppermute | solution.py:16
  13.4 1.0 collective-permute-done
  14.3 4.0 %collective-permute-start.1 = (f32[128,128]{1,0:T(8,128)S(1)}, f32[128,128]{1,0:T(8,128)S(1)}, u32[]{:S(2)}, u32[]{:S(2)}) collective-permute-start(f32[128,128]{1,0:T(8,128)S(1)} %add_bitcast_fusion.1), channel_id=1, source_target_pairs={{0,32},{32,64},{64,96},{96,128},{128,160},{160,192},{192,224},{224... | collective-permute-start | bytes 196616 | tf_op jit(solution)/shard_map/ppermute | solution.py:39
  18.3 1.3 collective-permute-done.1
  19.7 5.8 %collective-permute-start.2 = (f32[128,128]{1,0:T(8,128)S(1)}, f32[128,128]{1,0:T(8,128)S(1)}, u32[]{:S(2)}, u32[]{:S(2)}) collective-permute-start(f32[128,128]{1,0:T(8,128)S(1)} %add.79), channel_id=1, source_target_pairs={{0,64},{32,96},{64,128},{96,160},{128,192},{160,224},{192,256},{22... | collective-permute-start | bytes 196616 | tf_op jit(solution)/shard_map/ppermute | solution.py:39
  25.5 1.3 collective-permute-done.2
  26.8 12.1 %collective-permute-start.3 = (f32[128,128]{1,0:T(8,128)S(1)}, f32[128,128]{1,0:T(8,128)S(1)}, u32[]{:S(2)}, u32[]{:S(2)}) collective-permute-start(f32[128,128]{1,0:T(8,128)S(1)} %add.81), channel_id=1, source_target_pairs={{0,128},{32,160},{64,192},{96,224},{128,256},{160,288},{192,320},{... | collective-permute-start | bytes 196616 | tf_op jit(solution)/shard_map/ppermute | solution.py:39
  39.0 1.3 collective-permute-done.3
  40.3 8.7 %collective-permute-start.4 = (f32[128,128]{1,0:T(8,128)S(1)}, f32[128,128]{1,0:T(8,128)S(1)}, u32[]{:S(2)}, u32[]{:S(2)}) collective-permute-start(f32[128,128]{1,0:T(8,128)S(1)} %add.83), channel_id=1, source_target_pairs={{0,256},{32,288},{64,320},{96,352},{128,384},{160,416},{192,448},{... | collective-permute-start | bytes 196616 | tf_op jit(solution)/shard_map/ppermute | solution.py:39
  49.0 0.0 copy-done
  49.0 1.1 convolution_select_fusion.1
  50.1 0.2 collective-permute-done.4
  50.3 5.7 %collective-permute-start.5 = (f32[128,128]{1,0:T(8,128)S(1)}, f32[128,128]{1,0:T(8,128)S(1)}, u32[]{:S(2)}, u32[]{:S(2)}) collective-permute-start(f32[128,128]{1,0:T(8,128)S(1)} %add_add_fusion.1), channel_id=1, source_target_pairs={{0,16},{16,0},{1,17},{17,1},{2,18},{18,2},{3,19},{19,3},{4,20},{20... | collective-permute-start | bytes 196616 | tf_op jit(solution)/shard_map/ppermute | solution.py:16
  56.1 0.0 copy-done.1
  56.1 0.4 convolution_bitcast_fusion.2
  56.5 0.4 collective-permute-done.5
  56.9 0.3 multiply_reduce_fusion.1
  57.3 21.5 %all-gather.3.cloned.1.call-done = bf16[256,4096]{1,0:T(8,128)(2,1)} async-done(((bf16[256,256]{1,0:T(8,128)(2,1)}), bf16[256,4096]{1,0:T(8,128)(2,1)}) %all-gather.3.cloned.1.call-update) | async-done | bytes 2097168 | tf_op jit(solution)/shard_map/all_gather | solution.py:54
  78.8 74.4 %all-gather.5.cloned.1.call-done = bf16[256,4096]{1,0:T(8,128)(2,1)} async-done(((bf16[256,128]{1,0:T(8,128)(2,1)}), bf16[256,4096]{1,0:T(8,128)(2,1)}) %all-gather.5.cloned.1.call-update) | async-done | bytes 2097168 | tf_op jit(solution)/shard_map/all_gather | solution.py:57
  153.3 3.0 %multiply_reduce_fusion = (f32[256,2]{0,1:T(2,128)S(1)}, f32[256,256]{0,1:T(8,128)S(1)}) fusion(f32[256,2,128]{0,2,1:T(8,128)S(1)} %get-tuple-element.11, f32[256,2]{0,1:T(2,128)S(1)} %add_rsqrt_fusion, bf16[256,4096]{1,0:T(8,128)(2,1)} %all-gather.3.cloned.1.call-done, bf16[256,4096]{1,0:T(8,128)(2,1)} %all-gather.5.cloned.1.call-done), kind=kOutput, calls=%fused_computation.17 | convolution fusion | flops 537067008 | bytes 4722688 | tf_op jit(solution)/shard_map/dot_general | solution.py:55
  156.3 0.2 convolution_bitcast_fusion.6
  156.5 2.2 %collective-permute-start.6 = (f32[2,128,128]{2,1,0:T(8,128)S(1)}, f32[2,128,128]{2,1,0:T(8,128)S(1)}, u32[]{:S(2)}, u32[]{:S(2)}) collective-permute-start(f32[2,128,128]{2,1,0:T(8,128)S(1)} %convolution_bitcast_fusion.6), channel_id=1, source_target_pairs={{0,16},{16,0},{1,17},{17,1},{2,18},{18,2},{3,19},{19,3},{4,20},{20... | collective-permute-start | bytes 393224 | tf_op jit(solution)/shard_map/ppermute | solution.py:16
  158.7 1.0 collective-permute-done.6
  159.8 1.3 collective-permute-start.7
  161.1 0.3 fusion.35
  161.4 3.4 %collective-permute-done.7 = f32[128,128]{1,0:T(8,128)S(1)} collective-permute-done((f32[128,128]{1,0:T(8,128)S(1)}, f32[128,128]{1,0:T(8,128)S(1)}, u32[]{:S(2)}, u32[]{:S(2)}) %collective-permute-start.7) | collective-permute-done | bytes 65568 | tf_op jit(solution)/shard_map/ppermute | solution.py:39
  164.8 1.3 collective-permute-start.8
  166.1 0.3 convolution_select_fusion
  166.4 0.0 copy-start.2
  166.4 5.0 %collective-permute-done.8 = f32[128,128]{1,0:T(8,128)S(1)} collective-permute-done((f32[128,128]{1,0:T(8,128)S(1)}, f32[128,128]{1,0:T(8,128)S(1)}, u32[]{:S(2)}, u32[]{:S(2)}) %collective-permute-start.8) | collective-permute-done | bytes 65568 | tf_op jit(solution)/shard_map/ppermute | solution.py:39
  171.4 1.3 collective-permute-start.9
  172.7 0.4 convolution_bitcast_fusion.1
  173.2 7.2 %collective-permute-done.9 = f32[128,128]{1,0:T(8,128)S(1)} collective-permute-done((f32[128,128]{1,0:T(8,128)S(1)}, f32[128,128]{1,0:T(8,128)S(1)}, u32[]{:S(2)}, u32[]{:S(2)}) %collective-permute-start.9) | collective-permute-done | bytes 65568 | tf_op jit(solution)/shard_map/ppermute | solution.py:39
  180.4 1.3 collective-permute-start.10
  181.7 0.4 convolution_bitcast_fusion
  182.0 3.4 %collective-permute-done.10 = f32[128,128]{1,0:T(8,128)S(1)} collective-permute-done((f32[128,128]{1,0:T(8,128)S(1)}, f32[128,128]{1,0:T(8,128)S(1)}, u32[]{:S(2)}, u32[]{:S(2)}) %collective-permute-start.10) | collective-permute-done | bytes 65568 | tf_op jit(solution)/shard_map/ppermute | solution.py:39
  185.4 7.5 %collective-permute-start.11 = (f32[128,128]{1,0:T(8,128)S(1)}, f32[128,128]{1,0:T(8,128)S(1)}, u32[]{:S(2)}, u32[]{:S(2)}) collective-permute-start(f32[128,128]{1,0:T(8,128)S(1)} %add_add_fusion), channel_id=1, source_target_pairs={{0,16},{16,0},{1,17},{17,1},{2,18},{18,2},{3,19},{19,3},{4,20},{20... | collective-permute-start | bytes 196616 | tf_op jit(solution)/shard_map/ppermute | solution.py:16
  192.9 0.3 fusion.3
  193.2 0.8 copy.25
  194.0 0.0 collective-permute-done.11
  194.0 0.0 copy-done.2
  194.0 0.3 fusion.5
  194.3 0.8 copy.27
  195.1 0.3 fusion.4
  195.4 0.8 copy.26
  (16 shorter events, 0.2 us)
Async XLA Ops:
  7.2 41.8 %copy-start = (bf16[256,256]{1,0:T(8,128)(2,1)S(1)}, bf16[256,256]{1,0:T(8,128)(2,1)}, u32[]{:S(2)}) copy-start(bf16[256,256]{1,0:T(8,128)(2,1)} %param.5) | copy-start | bytes 393220
  7.2 48.9 %copy-start.1 = (bf16[256,256]{1,0:T(8,128)(2,1)S(1)}, bf16[256,256]{1,0:T(8,128)(2,1)}, u32[]{:S(2)}) copy-start(bf16[256,256]{1,0:T(8,128)(2,1)} %param.7) | copy-start | bytes 393220
  7.2 71.6 %all-gather.3.cloned.1.call-start = ((), (), s32[]{:S(2)}) async-start(), calls=%async_computation | async-start | bytes 2228224 | tf_op jit(solution)/shard_map/all_gather | solution.py:54
  7.9 145.3 %all-gather.5.cloned.1.call-start = ((), (), s32[]{:S(2)}) async-start(), calls=%async_computation.1 | async-start | bytes 2162688 | tf_op jit(solution)/shard_map/all_gather | solution.py:57
  10.8 3.6 %collective-permute-start = (f32[2,128,128]{2,1,0:T(8,128)S(1)}, f32[2,128,128]{2,1,0:T(8,128)S(1)}, u32[]{:S(2)}, u32[]{:S(2)}) collective-permute-start(f32[2,128,128]{2,1,0:T(8,128)S(1)} %fusion.9), channel_id=1, source_target_pairs={{0,16},{16,0},{1,17},{17,1},{2,18},{18,2},{3,19},{19,3},{4,20},{20... | collective-permute-start | bytes 393224 | tf_op jit(solution)/shard_map/ppermute | solution.py:16
  14.3 5.3 %collective-permute-start.1 = (f32[128,128]{1,0:T(8,128)S(1)}, f32[128,128]{1,0:T(8,128)S(1)}, u32[]{:S(2)}, u32[]{:S(2)}) collective-permute-start(f32[128,128]{1,0:T(8,128)S(1)} %add_bitcast_fusion.1), channel_id=1, source_target_pairs={{0,32},{32,64},{64,96},{96,128},{128,160},{160,192},{192,224},{224... | collective-permute-start | bytes 196616 | tf_op jit(solution)/shard_map/ppermute | solution.py:39
  19.7 7.1 %collective-permute-start.2 = (f32[128,128]{1,0:T(8,128)S(1)}, f32[128,128]{1,0:T(8,128)S(1)}, u32[]{:S(2)}, u32[]{:S(2)}) collective-permute-start(f32[128,128]{1,0:T(8,128)S(1)} %add.79), channel_id=1, source_target_pairs={{0,64},{32,96},{64,128},{96,160},{128,192},{160,224},{192,256},{22... | collective-permute-start | bytes 196616 | tf_op jit(solution)/shard_map/ppermute | solution.py:39
  26.8 13.5 %collective-permute-start.3 = (f32[128,128]{1,0:T(8,128)S(1)}, f32[128,128]{1,0:T(8,128)S(1)}, u32[]{:S(2)}, u32[]{:S(2)}) collective-permute-start(f32[128,128]{1,0:T(8,128)S(1)} %add.81), channel_id=1, source_target_pairs={{0,128},{32,160},{64,192},{96,224},{128,256},{160,288},{192,320},{... | collective-permute-start | bytes 196616 | tf_op jit(solution)/shard_map/ppermute | solution.py:39
  40.3 10.0 %collective-permute-start.4 = (f32[128,128]{1,0:T(8,128)S(1)}, f32[128,128]{1,0:T(8,128)S(1)}, u32[]{:S(2)}, u32[]{:S(2)}) collective-permute-start(f32[128,128]{1,0:T(8,128)S(1)} %add.83), channel_id=1, source_target_pairs={{0,256},{32,288},{64,320},{96,352},{128,384},{160,416},{192,448},{... | collective-permute-start | bytes 196616 | tf_op jit(solution)/shard_map/ppermute | solution.py:39
  50.3 6.6 %collective-permute-start.5 = (f32[128,128]{1,0:T(8,128)S(1)}, f32[128,128]{1,0:T(8,128)S(1)}, u32[]{:S(2)}, u32[]{:S(2)}) collective-permute-start(f32[128,128]{1,0:T(8,128)S(1)} %add_add_fusion.1), channel_id=1, source_target_pairs={{0,16},{16,0},{1,17},{17,1},{2,18},{18,2},{3,19},{19,3},{4,20},{20... | collective-permute-start | bytes 196616 | tf_op jit(solution)/shard_map/ppermute | solution.py:16
  156.5 3.2 %collective-permute-start.6 = (f32[2,128,128]{2,1,0:T(8,128)S(1)}, f32[2,128,128]{2,1,0:T(8,128)S(1)}, u32[]{:S(2)}, u32[]{:S(2)}) collective-permute-start(f32[2,128,128]{2,1,0:T(8,128)S(1)} %convolution_bitcast_fusion.6), channel_id=1, source_target_pairs={{0,16},{16,0},{1,17},{17,1},{2,18},{18,2},{3,19},{19,3},{4,20},{20... | collective-permute-start | bytes 393224 | tf_op jit(solution)/shard_map/ppermute | solution.py:16
  159.8 5.0 %collective-permute-start.7 = (f32[128,128]{1,0:T(8,128)S(1)}, f32[128,128]{1,0:T(8,128)S(1)}, u32[]{:S(2)}, u32[]{:S(2)}) collective-permute-start(f32[128,128]{1,0:T(8,128)S(1)} %add_bitcast_fusion), channel_id=1, source_target_pairs={{32,0},{64,32},{96,64},{128,96},{160,128},{192,160},{224,192},{256... | collective-permute-start | bytes 196616 | tf_op jit(solution)/shard_map/ppermute | solution.py:39
  164.8 6.6 %collective-permute-start.8 = (f32[128,128]{1,0:T(8,128)S(1)}, f32[128,128]{1,0:T(8,128)S(1)}, u32[]{:S(2)}, u32[]{:S(2)}) collective-permute-start(f32[128,128]{1,0:T(8,128)S(1)} %add.91), channel_id=1, source_target_pairs={{64,0},{96,32},{128,64},{160,96},{192,128},{224,160},{256,192},{28... | collective-permute-start | bytes 196616 | tf_op jit(solution)/shard_map/ppermute | solution.py:39
  166.4 27.6 %copy-start.2 = (bf16[256,256]{1,0:T(8,128)(2,1)S(1)}, bf16[256,256]{1,0:T(8,128)(2,1)}, u32[]{:S(2)}) copy-start(bf16[256,256]{1,0:T(8,128)(2,1)} %param.6) | copy-start | bytes 393220
  171.4 8.9 %collective-permute-start.9 = (f32[128,128]{1,0:T(8,128)S(1)}, f32[128,128]{1,0:T(8,128)S(1)}, u32[]{:S(2)}, u32[]{:S(2)}) collective-permute-start(f32[128,128]{1,0:T(8,128)S(1)} %add.93), channel_id=1, source_target_pairs={{128,0},{160,32},{192,64},{224,96},{256,128},{288,160},{320,192},{... | collective-permute-start | bytes 196616 | tf_op jit(solution)/shard_map/ppermute | solution.py:39
  180.4 5.0 %collective-permute-start.10 = (f32[128,128]{1,0:T(8,128)S(1)}, f32[128,128]{1,0:T(8,128)S(1)}, u32[]{:S(2)}, u32[]{:S(2)}) collective-permute-start(f32[128,128]{1,0:T(8,128)S(1)} %add.95), channel_id=1, source_target_pairs={{256,0},{288,32},{320,64},{352,96},{384,128},{416,160},{448,192},{... | collective-permute-start | bytes 196616 | tf_op jit(solution)/shard_map/ppermute | solution.py:39
  185.4 8.6 %collective-permute-start.11 = (f32[128,128]{1,0:T(8,128)S(1)}, f32[128,128]{1,0:T(8,128)S(1)}, u32[]{:S(2)}, u32[]{:S(2)}) collective-permute-start(f32[128,128]{1,0:T(8,128)S(1)} %add_add_fusion), channel_id=1, source_target_pairs={{0,16},{16,0},{1,17},{17,1},{2,18},{18,2},{3,19},{19,3},{4,20},{20... | collective-permute-start | bytes 196616 | tf_op jit(solution)/shard_map/ppermute | solution.py:16
Sparse Core Ops, SparseCore 0:
  11.0 67.7 all-gather.2
  80.9 72.3 all-gather.4
where the time goes:
time: 203 us
  waiting for transfers between devices  123 us (61%)
  starting transfers between devices  53.9 us (27%)
  between operations  14.3 us (7%)
  matrix products  8.44 us (4%)
  local copies, waits for them, and re-layouts  3.31 us (2%)
    all_gather x1, waiting for transfers between devices, local(): lax.all_gather(w_out, CTX, axis=1, tiled=True)  74.4 us
    ppermute x8, starting transfers between devices, ctx_scan(): arrived = lax.ppermute(window, CHIPS, pairs)  35.8 us
    ppermute x8, waiting for transfers between devices, ctx_scan(): arrived = lax.ppermute(window, CHIPS, pairs)  23 us
    all_gather x1, waiting for transfers between devices, local(): full_rows = lax.all_gather(grad_out, TP, axis=1, tiled=True)  21.5 us
    ppermute x4, starting transfers between devices, swap_cores(): return lax.ppermute(value, 'core', [(0, 1), (1, 0)])  18.1 us
  transfers between devices with their start and end apart: 14, of which 13 were waited for; matrix products, arithmetic and copies ran while one was open for 3% of the time, Pallas kernels for 0%

commit v1 on v0

--- a/solution.py
+++ b/solution.py
@@ -54,7 +54,7 @@
     full_rows = lax.all_gather(grad_out, TP, axis=1, tiled=True)
     grad_z = lax.dot_general(
         full_rows,
-        lax.all_gather(w_out, CTX, axis=1, tiled=True),
+        jnp.concatenate(lax.all_to_all(jnp.stack([w_out] * lax.axis_size(CTX)), CTX, 0, 0), axis=1),
         (((1,), (1,)), ((), ())),
         preferred_element_type=jnp.float32,
     )

time: 203 us -> 165 us (0.81)
  the two profiles are of different devices: /device:TPU:3 before, /device:TPU:17 now
where the time goes in v1:
time: 165 us; the launch traced here: 164 us
  waiting for transfers between devices  65.3 us (40%)
  starting transfers between devices  65.1 us (39%)
  between operations  14.4 us (9%)
  local copies, waits for them, and re-layouts  10.6 us (6%)
  matrix products  6.72 us (4%)
  other arithmetic  1.72 us (1%)
    ppermute x8, waiting for transfers between devices, ctx_scan(): arrived = lax.ppermute(window, CHIPS, pairs)  61.8 us
    ppermute x8, starting transfers between devices, ctx_scan(): arrived = lax.ppermute(window, CHIPS, pairs)  37.6 us
    ppermute x4, starting transfers between devices, swap_cores(): return lax.ppermute(value, 'core', [(0, 1), (1, 0)])  15.1 us
    all_to_all x1, starting transfers between devices, local(): lax.all_to_all(jnp.stack([w_out] * lax.axis_size(CTX)), CTX, 0, 0)  12.3 us
  transfers between devices with their start and end apart: 14, of which 11 were waited for; matrix products, arithmetic and copies ran while one was open for 7% of the time, Pallas kernels for 0%

profile of v1, /device:TPU:17, one launch (start us, length us, event | category | flops | bytes accessed | tf_op | source)
XLA Modules:
  0.0 163.9 jit_solution(16346426516387358921)
XLA Ops:
  7.2 0.0 copy-start
  7.2 2.7 %stack.17 = bf16[32,256,128]{2,1,0:T(8,128)(2,1)} broadcast(bf16[256,128]{1,0:T(8,128)(2,1)} %param.9), dimensions={1,2} | broadcast | bytes 2162688 | tf_op jit(solution)/shard_map/stack | solution.py:57
  9.8 12.3 %all-to-all-start = ((bf16[32,256,128]{2,1,0:T(8,128)(2,1)}), bf16[32,256,128]{2,1,0:T(8,128)(2,1)S(1)}, u32[]{:S(2)}, u32[]{:S(2)}) async-start(bf16[32,256,128]{2,1,0:T(8,128)(2,1)} %stack.17), calls=%async_computation | async-start | bytes 4194304 | tf_op jit(solution)/shard_map/all_to_all | solution.py:57
  22.1 0.0 all-gather.2.cloned.1.call-start
  22.2 0.7 all-gather.2.cloned.1.call-update
  22.9 0.0 copy-done.2
  22.9 0.1 copy.97
  23.0 0.0 copy-done.1
  23.0 0.2 fusion.11
  23.2 2.1 %collective-permute-start = (f32[2,128,128]{2,1,0:T(8,128)S(1)}, f32[2,128,128]{2,1,0:T(8,128)S(1)}, u32[]{:S(2)}, u32[]{:S(2)}) collective-permute-start(f32[2,128,128]{2,1,0:T(8,128)S(1)} %fusion.11), channel_id=1, source_target_pairs={{0,16},{16,0},{1,17},{17,1},{2,18},{18,2},{3,19},{19,3},{4,20},{20... | collective-permute-start | bytes 393224 | tf_op jit(solution)/shard_map/ppermute | solution.py:16
  25.3 1.1 collective-permute-done
  26.4 3.3 %collective-permute-start.1 = (f32[128,128]{1,0:T(8,128)S(1)}, f32[128,128]{1,0:T(8,128)S(1)}, u32[]{:S(2)}, u32[]{:S(2)}) collective-permute-start(f32[128,128]{1,0:T(8,128)S(1)} %add_bitcast_fusion.1), channel_id=1, source_target_pairs={{0,32},{32,64},{64,96},{96,128},{128,160},{160,192},{192,224},{224... | collective-permute-start | bytes 196616 | tf_op jit(solution)/shard_map/ppermute | solution.py:39
  29.7 39.2 %collective-permute-done.1 = f32[128,128]{1,0:T(8,128)S(1)} collective-permute-done((f32[128,128]{1,0:T(8,128)S(1)}, f32[128,128]{1,0:T(8,128)S(1)}, u32[]{:S(2)}, u32[]{:S(2)}) %collective-permute-start.1) | collective-permute-done | bytes 65568 | tf_op jit(solution)/shard_map/ppermute | solution.py:39
  69.0 6.0 %collective-permute-start.2 = (f32[128,128]{1,0:T(8,128)S(1)}, f32[128,128]{1,0:T(8,128)S(1)}, u32[]{:S(2)}, u32[]{:S(2)}) collective-permute-start(f32[128,128]{1,0:T(8,128)S(1)} %add.79), channel_id=1, source_target_pairs={{0,64},{32,96},{64,128},{96,160},{128,192},{160,224},{192,256},{22... | collective-permute-start | bytes 196616 | tf_op jit(solution)/shard_map/ppermute | solution.py:39
  74.9 1.3 collective-permute-done.2
  76.3 9.0 %collective-permute-start.3 = (f32[128,128]{1,0:T(8,128)S(1)}, f32[128,128]{1,0:T(8,128)S(1)}, u32[]{:S(2)}, u32[]{:S(2)}) collective-permute-start(f32[128,128]{1,0:T(8,128)S(1)} %add.81), channel_id=1, source_target_pairs={{0,128},{32,160},{64,192},{96,224},{128,256},{160,288},{192,320},{... | collective-permute-start | bytes 196616 | tf_op jit(solution)/shard_map/ppermute | solution.py:39
  85.3 0.0 copy-start.8
  85.3 1.3 collective-permute-done.3
  86.6 14.1 %collective-permute-start.4 = (f32[128,128]{1,0:T(8,128)S(1)}, f32[128,128]{1,0:T(8,128)S(1)}, u32[]{:S(2)}, u32[]{:S(2)}) collective-permute-start(f32[128,128]{1,0:T(8,128)S(1)} %add.83), channel_id=1, source_target_pairs={{0,256},{32,288},{64,320},{96,352},{128,384},{160,416},{192,448},{... | collective-permute-start | bytes 196616 | tf_op jit(solution)/shard_map/ppermute | solution.py:39
  100.7 0.0 copy-done
  100.7 0.2 convolution_select_fusion.1
  100.9 1.1 collective-permute-done.4
  102.0 0.6 add_add_fusion.1
  102.6 0.0 copy-done.8
  102.7 3.4 %collective-permute-start.5 = (f32[128,128]{1,0:T(8,128)}, f32[128,128]{1,0:T(8,128)}, u32[]{:S(2)}, u32[]{:S(2)}) collective-permute-start(f32[128,128]{1,0:T(8,128)} %add_add_fusion.1), channel_id=1, source_target_pairs={{0,16},{16,0},{1,17},{17,1},{2,18},{18,2},{3,19},{19,3},{4,20},{20... | collective-permute-start | bytes 196616 | tf_op jit(solution)/shard_map/ppermute | solution.py:16
  106.1 0.4 convolution_bitcast_fusion.2
  106.5 0.8 collective-permute-done.5
  107.3 0.9 select_bitcast_fusion.3
  108.2 0.0 copy-start.4
  108.2 0.0 copy-start.6
  108.2 1.1 multiply_reduce_fusion.1
  109.3 0.0 copy-done.4
  109.3 0.0 copy-done.6
  109.3 0.0 all-to-all-done
  109.3 2.7 %copy.35 = bf16[256,32,128]{2,1,0:T(8,128)(2,1)} copy(bf16[256,32,128]{2,0,1:T(8,128)(2,1)S(1)} %bitcast.117) | data formatting | bytes 4194304 | tf_op jit(solution)/shard_map/reshape | solution.py:57
  112.0 2.9 %dot_general.47 = bf16[2,128,4096]{2,1,0:T(8,128)(2,1)S(1)} reshape(bf16[256,32,128]{2,1,0:T(8,128)(2,1)} %copy.35) | data formatting | bytes 4194304 | tf_op jit(solution)/shard_map/dot_general | solution.py:55
  114.8 0.0 all-gather.2.cloned.1.call-done
  114.9 2.3 %multiply_reduce_fusion = (f32[256,2]{0,1:T(2,128)S(1)}, f32[256,2,128]{0,2,1:T(8,128)S(1)}) fusion(f32[256,2,128]{0,2,1:T(8,128)S(1)} %copy-done.3, f32[256,2]{0,1:T(2,128)S(1)} %add_rsqrt_fusion, bf16[2,128,4096]{2,1,0:T(8,128)(2,1)S(1)} %dot_general.47, bf16[256,4096]{1,0:T(8,128)(2,1)} %all-gather.2.cloned.1.call-done), kind=kOutput, calls=%fused_computation.19 | convolution fusion | flops 537067008 | bytes 4722688 | tf_op jit(solution)/shard_map/dot_general | solution.py:55
  117.2 0.0 copy-start.9
  117.3 0.2 convolution_bitcast_fusion.6
  117.5 2.3 %collective-permute-start.6 = (f32[2,128,128]{2,1,0:T(8,128)S(1)}, f32[2,128,128]{2,1,0:T(8,128)S(1)}, u32[]{:S(2)}, u32[]{:S(2)}) collective-permute-start(f32[2,128,128]{2,1,0:T(8,128)S(1)} %convolution_bitcast_fusion.6), channel_id=1, source_target_pairs={{0,16},{16,0},{1,17},{17,1},{2,18},{18,2},{3,19},{19,3},{4,20},{20... | collective-permute-start | bytes 393224 | tf_op jit(solution)/shard_map/ppermute | solution.py:16
  119.8 1.0 collective-permute-done.6
  120.8 0.0 copy-start.5
  120.8 0.0 copy-start.7
  120.8 1.4 collective-permute-start.7
  122.2 0.3 fusion.37
  122.6 3.4 %collective-permute-done.7 = f32[128,128]{1,0:T(8,128)S(1)} collective-permute-done((f32[128,128]{1,0:T(8,128)S(1)}, f32[128,128]{1,0:T(8,128)S(1)}, u32[]{:S(2)}, u32[]{:S(2)}) %collective-permute-start.7) | collective-permute-done | bytes 65568 | tf_op jit(solution)/shard_map/ppermute | solution.py:39
  126.0 1.3 collective-permute-start.8
  127.3 0.3 convolution_select_fusion
  127.6 5.0 %collective-permute-done.8 = f32[128,128]{1,0:T(8,128)S(1)} collective-permute-done((f32[128,128]{1,0:T(8,128)S(1)}, f32[128,128]{1,0:T(8,128)S(1)}, u32[]{:S(2)}, u32[]{:S(2)}) %collective-permute-start.8) | collective-permute-done | bytes 65568 | tf_op jit(solution)/shard_map/ppermute | solution.py:39
  132.6 1.3 collective-permute-start.9
  133.9 0.4 convolution_bitcast_fusion
  134.2 7.3 %collective-permute-done.9 = f32[128,128]{1,0:T(8,128)S(1)} collective-permute-done((f32[128,128]{1,0:T(8,128)S(1)}, f32[128,128]{1,0:T(8,128)S(1)}, u32[]{:S(2)}, u32[]{:S(2)}) %collective-permute-start.9) | collective-permute-done | bytes 65568 | tf_op jit(solution)/shard_map/ppermute | solution.py:39
  141.5 1.3 collective-permute-start.10
  142.8 0.4 convolution_bitcast_fusion.1
  143.3 3.3 %collective-permute-done.10 = f32[128,128]{1,0:T(8,128)S(1)} collective-permute-done((f32[128,128]{1,0:T(8,128)S(1)}, f32[128,128]{1,0:T(8,128)S(1)}, u32[]{:S(2)}, u32[]{:S(2)}) %collective-permute-start.10) | collective-permute-done | bytes 65568 | tf_op jit(solution)/shard_map/ppermute | solution.py:39
  146.6 7.3 %collective-permute-start.11 = (f32[128,128]{1,0:T(8,128)S(1)}, f32[128,128]{1,0:T(8,128)S(1)}, u32[]{:S(2)}, u32[]{:S(2)}) collective-permute-start(f32[128,128]{1,0:T(8,128)S(1)} %add_add_fusion), channel_id=1, source_target_pairs={{0,16},{16,0},{1,17},{17,1},{2,18},{18,2},{3,19},{19,3},{4,20},{20... | collective-permute-start | bytes 196616 | tf_op jit(solution)/shard_map/ppermute | solution.py:16
  153.8 0.3 fusion.5
  154.1 0.8 copy.46
  154.9 0.0 collective-permute-done.11
  154.9 0.3 fusion.7
  155.2 0.8 copy.48
  156.0 0.3 fusion.6
  156.3 0.8 copy.47
  (21 shorter events, 0.2 us)
Async XLA Ops:
  7.2 93.5 %copy-start = (bf16[256,256]{1,0:T(8,128)(2,1)S(1)}, bf16[256,256]{1,0:T(8,128)(2,1)}, u32[]{:S(2)}) copy-start(bf16[256,256]{1,0:T(8,128)(2,1)} %param.5) | copy-start | bytes 393220
  9.8 13.0 %copy-start.2 = (bf16[256,256]{1,0:T(8,128)(2,1)S(1)}, bf16[256,256]{1,0:T(8,128)(2,1)}, u32[]{:S(2)}) copy-start(bf16[256,256]{1,0:T(8,128)(2,1)} %param.6) | copy-start | bytes 393220
  9.8 13.2 %copy-start.1 = (bf16[256,256]{1,0:T(8,128)(2,1)S(1)}, bf16[256,256]{1,0:T(8,128)(2,1)}, u32[]{:S(2)}) copy-start(bf16[256,256]{1,0:T(8,128)(2,1)} %param.7) | copy-start | bytes 393220
  9.8 99.5 %all-to-all-start = ((bf16[32,256,128]{2,1,0:T(8,128)(2,1)}), bf16[32,256,128]{2,1,0:T(8,128)(2,1)S(1)}, u32[]{:S(2)}, u32[]{:S(2)}) async-start(bf16[32,256,128]{2,1,0:T(8,128)(2,1)} %stack.17), calls=%async_computation | async-start | bytes 4194304 | tf_op jit(solution)/shard_map/all_to_all | solution.py:57
  22.1 92.7 %all-gather.2.cloned.1.call-start = ((), (), s32[]{:S(2)}) async-start(), calls=%async_computation.1 | async-start | bytes 2228224 | tf_op jit(solution)/shard_map/all_gather | solution.py:54
  23.2 3.2 %collective-permute-start = (f32[2,128,128]{2,1,0:T(8,128)S(1)}, f32[2,128,128]{2,1,0:T(8,128)S(1)}, u32[]{:S(2)}, u32[]{:S(2)}) collective-permute-start(f32[2,128,128]{2,1,0:T(8,128)S(1)} %fusion.11), channel_id=1, source_target_pairs={{0,16},{16,0},{1,17},{17,1},{2,18},{18,2},{3,19},{19,3},{4,20},{20... | collective-permute-start | bytes 393224 | tf_op jit(solution)/shard_map/ppermute | solution.py:16
  26.4 42.5 %collective-permute-start.1 = (f32[128,128]{1,0:T(8,128)S(1)}, f32[128,128]{1,0:T(8,128)S(1)}, u32[]{:S(2)}, u32[]{:S(2)}) collective-permute-start(f32[128,128]{1,0:T(8,128)S(1)} %add_bitcast_fusion.1), channel_id=1, source_target_pairs={{0,32},{32,64},{64,96},{96,128},{128,160},{160,192},{192,224},{224... | collective-permute-start | bytes 196616 | tf_op jit(solution)/shard_map/ppermute | solution.py:39
  69.0 7.3 %collective-permute-start.2 = (f32[128,128]{1,0:T(8,128)S(1)}, f32[128,128]{1,0:T(8,128)S(1)}, u32[]{:S(2)}, u32[]{:S(2)}) collective-permute-start(f32[128,128]{1,0:T(8,128)S(1)} %add.79), channel_id=1, source_target_pairs={{0,64},{32,96},{64,128},{96,160},{128,192},{160,224},{192,256},{22... | collective-permute-start | bytes 196616 | tf_op jit(solution)/shard_map/ppermute | solution.py:39
  76.3 10.3 %collective-permute-start.3 = (f32[128,128]{1,0:T(8,128)S(1)}, f32[128,128]{1,0:T(8,128)S(1)}, u32[]{:S(2)}, u32[]{:S(2)}) collective-permute-start(f32[128,128]{1,0:T(8,128)S(1)} %add.81), channel_id=1, source_target_pairs={{0,128},{32,160},{64,192},{96,224},{128,256},{160,288},{192,320},{... | collective-permute-start | bytes 196616 | tf_op jit(solution)/shard_map/ppermute | solution.py:39
  85.3 17.4 %copy-start.8 = (pred[256,256]{1,0:T(8,128)(4,1)}, pred[256,256]{1,0:T(8,128)(4,1)S(1)}, u32[]{:S(2)}) copy-start(pred[256,256]{1,0:T(8,128)(4,1)S(1)} %iota_compare_fusion) | copy-start | bytes 196612
  86.6 15.4 %collective-permute-start.4 = (f32[128,128]{1,0:T(8,128)S(1)}, f32[128,128]{1,0:T(8,128)S(1)}, u32[]{:S(2)}, u32[]{:S(2)}) collective-permute-start(f32[128,128]{1,0:T(8,128)S(1)} %add.83), channel_id=1, source_target_pairs={{0,256},{32,288},{64,320},{96,352},{128,384},{160,416},{192,448},{... | collective-permute-start | bytes 196616 | tf_op jit(solution)/shard_map/ppermute | solution.py:39
  102.7 4.7 %collective-permute-start.5 = (f32[128,128]{1,0:T(8,128)}, f32[128,128]{1,0:T(8,128)}, u32[]{:S(2)}, u32[]{:S(2)}) collective-permute-start(f32[128,128]{1,0:T(8,128)} %add_add_fusion.1), channel_id=1, source_target_pairs={{0,16},{16,0},{1,17},{17,1},{2,18},{18,2},{3,19},{19,3},{4,20},{20... | collective-permute-start | bytes 196616 | tf_op jit(solution)/shard_map/ppermute | solution.py:16
  108.2 1.1 copy-start.4
  108.2 1.1 copy-start.6
  112.0 2.9 %copy-start.3 = (f32[256,2,128]{0,2,1:T(8,128)S(1)}, f32[256,2,128]{0,2,1:T(8,128)}, u32[]{:S(2)}) copy-start(f32[256,2,128]{0,2,1:T(8,128)} %get-tuple-element.14) | copy-start | bytes 786436
  117.2 10.0 %copy-start.9 = (pred[256,256]{1,0:T(8,128)(4,1)S(1)}, pred[256,256]{1,0:T(8,128)(4,1)}, u32[]{:S(2)}) copy-start(pred[256,256]{1,0:T(8,128)(4,1)} %copy-done.8) | copy-start | bytes 196612
  117.5 3.2 %collective-permute-start.6 = (f32[2,128,128]{2,1,0:T(8,128)S(1)}, f32[2,128,128]{2,1,0:T(8,128)S(1)}, u32[]{:S(2)}, u32[]{:S(2)}) collective-permute-start(f32[2,128,128]{2,1,0:T(8,128)S(1)} %convolution_bitcast_fusion.6), channel_id=1, source_target_pairs={{0,16},{16,0},{1,17},{17,1},{2,18},{18,2},{3,19},{19,3},{4,20},{20... | collective-permute-start | bytes 393224 | tf_op jit(solution)/shard_map/ppermute | solution.py:16
  120.8 33.0 %copy-start.5 = (f32[1,128,128]{2,1,0:T(8,128)S(1)}, f32[1,128,128]{2,1,0:T(8,128)}, u32[]{:S(2)}) copy-start(f32[1,128,128]{2,1,0:T(8,128)} %copy-done.4) | copy-start | bytes 196612
  120.8 33.0 %copy-start.7 = (f32[1,128,128]{2,1,0:T(8,128)S(1)}, f32[1,128,128]{2,1,0:T(8,128)}, u32[]{:S(2)}) copy-start(f32[1,128,128]{2,1,0:T(8,128)} %copy-done.6) | copy-start | bytes 196612
  120.8 5.1 %collective-permute-start.7 = (f32[128,128]{1,0:T(8,128)S(1)}, f32[128,128]{1,0:T(8,128)S(1)}, u32[]{:S(2)}, u32[]{:S(2)}) collective-permute-start(f32[128,128]{1,0:T(8,128)S(1)} %add_bitcast_fusion), channel_id=1, source_target_pairs={{32,0},{64,32},{96,64},{128,96},{160,128},{192,160},{224,192},{256... | collective-permute-start | bytes 196616 | tf_op jit(solution)/shard_map/ppermute | solution.py:39
  126.0 6.6 %collective-permute-start.8 = (f32[128,128]{1,0:T(8,128)S(1)}, f32[128,128]{1,0:T(8,128)S(1)}, u32[]{:S(2)}, u32[]{:S(2)}) collective-permute-start(f32[128,128]{1,0:T(8,128)S(1)} %add.91), channel_id=1, source_target_pairs={{64,0},{96,32},{128,64},{160,96},{192,128},{224,160},{256,192},{28... | collective-permute-start | bytes 196616 | tf_op jit(solution)/shard_map/ppermute | solution.py:39
  132.6 8.9 %collective-permute-start.9 = (f32[128,128]{1,0:T(8,128)S(1)}, f32[128,128]{1,0:T(8,128)S(1)}, u32[]{:S(2)}, u32[]{:S(2)}) collective-permute-start(f32[128,128]{1,0:T(8,128)S(1)} %add.93), channel_id=1, source_target_pairs={{128,0},{160,32},{192,64},{224,96},{256,128},{288,160},{320,192},{... | collective-permute-start | bytes 196616 | tf_op jit(solution)/shard_map/ppermute | solution.py:39
  141.5 5.0 %collective-permute-start.10 = (f32[128,128]{1,0:T(8,128)S(1)}, f32[128,128]{1,0:T(8,128)S(1)}, u32[]{:S(2)}, u32[]{:S(2)}) collective-permute-start(f32[128,128]{1,0:T(8,128)S(1)} %add.95), channel_id=1, source_target_pairs={{256,0},{288,32},{320,64},{352,96},{384,128},{416,160},{448,192},{... | collective-permute-start | bytes 196616 | tf_op jit(solution)/shard_map/ppermute | solution.py:39
  146.6 8.3 %collective-permute-start.11 = (f32[128,128]{1,0:T(8,128)S(1)}, f32[128,128]{1,0:T(8,128)S(1)}, u32[]{:S(2)}, u32[]{:S(2)}) collective-permute-start(f32[128,128]{1,0:T(8,128)S(1)} %add_add_fusion), channel_id=1, source_target_pairs={{0,16},{16,0},{1,17},{17,1},{2,18},{18,2},{3,19},{19,3},{4,20},{20... | collective-permute-start | bytes 196616 | tf_op jit(solution)/shard_map/ppermute | solution.py:16
Sparse Core Ops, SparseCore 0:
  25.9 64.3 all-gather.1
